TPU v7x, 256 devices: a whole 4x4x8 slice. The times are simulated.
256 devices in a mesh: uly: 8 (over x_hi, y), blk: 32 (over x_lo, z, core).
Axes of the slice: x: 4 (x_hi: 2, x_lo: 2; x = x_hi * 2 + x_lo), y: 4, z: 8, core: 2. Of those that a mesh axis runs over, the one named last changes fastest.
Arguments:
- queries: bfloat16 [16384, 2048], P(('uly', 'blk')), may hold values from -6 to 6
- key_vector_rows: bfloat16 [16384, 256], P(('uly', 'blk')), may hold values from -6 to 6
- value_vector_rows: bfloat16 [16384, 256], P(('uly', 'blk')), may hold values from -6 to 6
- out_grad: bfloat16 [16384, 2048], P(('uly', 'blk')), may hold values from -6 to 6
- block_list: int32 [16, 128, 8], P('uly'), may hold values from 0 to 127, as said below
Outputs:
- attended: bfloat16 [16384, 2048], P(('uly', 'blk'))
- query_grad: bfloat16 [16384, 2048], P(('uly', 'blk'))
- gradient_keys: bfloat16 [16384, 256], P(('uly', 'blk'))
- gradient_values: bfloat16 [16384, 256], P(('uly', 'blk'))
Inputs may be any that keep to these rules, and one draw needn't show every extreme that they name: block_list[h, i] names key blocks for query block i of head h: its first entry is always i itself, every entry is at most i, and a block may be named several times.
All inputs are finite; a program needn't handle non-finite values.
Results may differ from a plain program's by a relative error of at most 0.039.
Values may be sent and summed in bfloat16 or wider, within the bound.
No kernel may reach another device: no remote copies, remote signals or barrier semaphores. Data moves between devices by JAX's collectives and lax.ppermute only.
A program may use at most 128 MiB of HBM per device.

v0:
```python
import math
import jax
import jax.numpy as jnp
from jax import lax
from jax.sharding import PartitionSpec as P

KEY_VALUE_HEADS = 2
HEAD_SIZE = 128
BLOCK = 128


def body(queries, key_vector_rows, value_vector_rows, out_grad, block_list):
    ulysses_width = lax.axis_size("uly")
    cycle_size = lax.axis_size("blk")
    segment_length = queries.shape[0]
    heads_dev = block_list.shape[0]
    list_len = block_list.shape[2]
    head_width = heads_dev * HEAD_SIZE
    copy_count = ulysses_width // KEY_VALUE_HEADS
    cycle_index = lax.axis_index("blk")
    score_scale = 1.0 / math.sqrt(HEAD_SIZE)
    sub_length = min(segment_length, BLOCK)
    sub_count = segment_length // sub_length
    unit_len = min(segment_length, BLOCK)
    units_per_block = BLOCK // unit_len
    units_per_segment = segment_length // unit_len
    total_tokens = segment_length * ulysses_width * cycle_size
    units_total = total_tokens // unit_len
    query_slots = queries.reshape(segment_length, ulysses_width, head_width)
    grad_slots = out_grad.reshape(segment_length, ulysses_width, head_width)
    kv_local = jnp.concatenate(
        [
            key_vector_rows.reshape(segment_length, KEY_VALUE_HEADS, HEAD_SIZE),
            value_vector_rows.reshape(segment_length, KEY_VALUE_HEADS, HEAD_SIZE),
        ],
        axis=2,
    )
    kv_slots = jnp.repeat(kv_local, copy_count, axis=1)
    query_all, kv_mine, grad_all = (
        lax.all_to_all(query_slots, "uly", split_axis=1, concat_axis=0, tiled=True),
        lax.all_to_all(kv_slots, "uly", split_axis=1, concat_axis=0, tiled=True),
        lax.all_to_all(grad_slots, "uly", split_axis=1, concat_axis=0, tiled=True),
    )
    keys_all = lax.all_gather(kv_mine[:, 0, :], "blk", axis=0, tiled=True)
    item_count = heads_dev * ulysses_width * sub_count
    query_items = (
        query_all.reshape(ulysses_width, sub_count, sub_length, heads_dev, HEAD_SIZE)
        .transpose(3, 0, 1, 2, 4)
        .reshape(item_count, sub_length, HEAD_SIZE)
    )
    grad_items = (
        grad_all.reshape(ulysses_width, sub_count, sub_length, heads_dev, HEAD_SIZE)
        .transpose(3, 0, 1, 2, 4)
        .reshape(item_count, sub_length, HEAD_SIZE)
    )
    item_ids = jnp.arange(item_count, dtype=jnp.int32)
    head_ids = item_ids // (ulysses_width * sub_count)
    slot_ids = item_ids // sub_count % ulysses_width
    sub_ids = item_ids % sub_count
    segments = slot_ids * cycle_size + cycle_index
    first_pos = segments * segment_length + sub_ids * sub_length
    query_block = first_pos // BLOCK
    entries = block_list[head_ids, query_block]
    earlier = jnp.arange(list_len)[:, None] > jnp.arange(list_len)[None, :]
    repeated = jnp.any((entries[:, :, None] == entries[:, None, :]) & earlier[None, :, :], axis=2)
    offsets = jnp.arange(BLOCK, dtype=jnp.int32)
    key_pos = (entries[:, :, None] * BLOCK + offsets[None, None, :]).reshape(
        item_count, list_len * BLOCK
    )
    live_keys = jnp.repeat(jnp.logical_not(repeated), BLOCK, axis=1)
    query_pos = first_pos[:, None] + jnp.arange(sub_length, dtype=jnp.int32)[None, :]
    allowed = (key_pos[:, None, :] <= query_pos[:, :, None]) & live_keys[:, None, :]
    unit_count = list_len * units_per_block
    natural_units = (
        entries[:, :, None] * units_per_block
        + jnp.arange(units_per_block, dtype=jnp.int32)[None, None, :]
    ).reshape(item_count, unit_count)
    unit_seg = natural_units // units_per_segment
    canon_units = (
        unit_seg % cycle_size * ulysses_width + unit_seg // cycle_size
    ) * units_per_segment + natural_units % units_per_segment
    keys_units = keys_all.reshape(units_total, unit_len * 2 * HEAD_SIZE)
    unit_iota = jnp.arange(units_total, dtype=jnp.int32)
    per_step = min(item_count, max(1, 512 // sub_length))
    step_count = item_count // per_step
    key_len = list_len * BLOCK

    def group_step(grad_acc, group_data):
        query_group, grad_group, fetch_group, canon_group, mask_group = group_data
        fetch_table = (fetch_group.reshape(-1)[:, None] == unit_iota[None, :]).astype(jnp.bfloat16)
        gathered = (
            jnp.dot(fetch_table, keys_units, preferred_element_type=jnp.float32)
            .astype(jnp.bfloat16)
            .reshape(per_step, key_len, 2 * HEAD_SIZE)
        )
        key_group = gathered[:, :, :HEAD_SIZE]
        value_group = gathered[:, :, HEAD_SIZE:]
        scores = (
            jnp.einsum("nqd,nkd->nqk", query_group, key_group, preferred_element_type=jnp.float32)
            * score_scale
        )
        masked = jnp.where(mask_group, scores, -1e30)
        row_max = jnp.max(masked, axis=2, keepdims=True)
        row_sum = jnp.sum(
            jnp.where(mask_group, jnp.exp(masked - row_max), 0.0), axis=2, keepdims=True
        )
        log_sum = row_max + jnp.log(row_sum)
        weights = jnp.where(mask_group, jnp.exp(masked - log_sum), 0.0)
        weights_low = weights.astype(jnp.bfloat16)
        out_group = jnp.einsum(
            "nqk,nkd->nqd", weights_low, value_group, preferred_element_type=jnp.float32
        ).astype(jnp.bfloat16)
        row_dot = jnp.sum(
            grad_group.astype(jnp.float32) * out_group.astype(jnp.float32), axis=2, keepdims=True
        )
        grad_weights = jnp.einsum(
            "nqd,nkd->nqk", grad_group, value_group, preferred_element_type=jnp.float32
        )
        score_grad = (weights * (grad_weights - row_dot) * score_scale).astype(jnp.bfloat16)
        query_group_grad = jnp.einsum(
            "nqk,nkd->nqd", score_grad, key_group, preferred_element_type=jnp.float32
        ).astype(jnp.bfloat16)
        key_portion = jnp.einsum(
            "nqk,nqd->nkd", score_grad, query_group, preferred_element_type=jnp.float32
        )
        value_portion = jnp.einsum(
            "nqk,nqd->nkd", weights_low, grad_group, preferred_element_type=jnp.float32
        )
        both_parts = jnp.concatenate([key_portion, value_portion], axis=2).reshape(
            per_step * unit_count, unit_len * 2 * HEAD_SIZE
        )
        place_table = (canon_group.reshape(-1)[:, None] == unit_iota[None, :]).astype(jnp.float32)
        grad_acc = grad_acc + jnp.dot(
            place_table.T,
            both_parts,
            preferred_element_type=jnp.float32,
            precision=lax.Precision.HIGHEST,
        )
        return (grad_acc, (out_group, query_group_grad))

    empty_grad = jnp.zeros((units_total, unit_len * 2 * HEAD_SIZE), jnp.float32)
    scan_inputs = (
        query_items.reshape(step_count, per_step, sub_length, HEAD_SIZE),
        grad_items.reshape(step_count, per_step, sub_length, HEAD_SIZE),
        canon_units.reshape(step_count, per_step, unit_count),
        canon_units.reshape(step_count, per_step, unit_count),
        allowed.reshape(step_count, per_step, sub_length, key_len),
    )
    unit_grads, item_outputs = lax.scan(group_step, empty_grad, scan_inputs)
    kv_grad_all = unit_grads.reshape(total_tokens, 2 * HEAD_SIZE)
    out_items = (
        item_outputs[0]
        .reshape(heads_dev, ulysses_width, sub_count, sub_length, HEAD_SIZE)
        .transpose(1, 2, 3, 0, 4)
        .reshape(ulysses_width * segment_length, 1, head_width)
    )
    qgrad_items = (
        item_outputs[1]
        .reshape(heads_dev, ulysses_width, sub_count, sub_length, HEAD_SIZE)
        .transpose(1, 2, 3, 0, 4)
        .reshape(ulysses_width * segment_length, 1, head_width)
    )
    attended_back, qgrad_back = (
        lax.all_to_all(out_items, "uly", split_axis=0, concat_axis=1, tiled=True),
        lax.all_to_all(qgrad_items, "uly", split_axis=0, concat_axis=1, tiled=True),
    )
    attended = attended_back.reshape(segment_length, ulysses_width * head_width)
    query_grad = qgrad_back.reshape(segment_length, ulysses_width * head_width)
    owned = lax.psum_scatter(kv_grad_all, "blk", scatter_dimension=0, tiled=True)
    result_tuple = lax.all_to_all(
        owned.reshape(ulysses_width * segment_length, 1, 2 * HEAD_SIZE),
        "uly",
        split_axis=0,
        concat_axis=1,
        tiled=True,
    )
    summed_total = result_tuple.reshape(
        segment_length, KEY_VALUE_HEADS, copy_count, 2 * HEAD_SIZE
    ).sum(axis=2)
    gradient_keys = (
        summed_total[:, :, :HEAD_SIZE]
        .reshape(segment_length, KEY_VALUE_HEADS * HEAD_SIZE)
        .astype(jnp.bfloat16)
    )
    gradient_values = (
        summed_total[:, :, HEAD_SIZE:]
        .reshape(segment_length, KEY_VALUE_HEADS * HEAD_SIZE)
        .astype(jnp.bfloat16)
    )
    return (attended, query_grad, gradient_keys, gradient_values)


def solution(mesh):
    in_specs = (
        P(("uly", "blk"), None),
        P(("uly", "blk"), None),
        P(("uly", "blk"), None),
        P(("uly", "blk"), None),
        P("uly", None, None),
    )
    out_specs = (
        P(("uly", "blk"), None),
        P(("uly", "blk"), None),
        P(("uly", "blk"), None),
        P(("uly", "blk"), None),
    )
    return jax.shard_map(body, mesh=mesh, in_specs=in_specs, out_specs=out_specs, check_vma=False)
```

profile of v0, /device:TPU:0, one launch (start us, length us, event | category | flops | bytes accessed | tf_op | source)
XLA Modules:
  0.0 419.6 jit_solution(4855047830497179188)
XLA Ops:
  8.9 13.9 %all_to_all.90 = bf16[64,8,256]{2,0,1:T(8,128)(2,1)} all-to-all(bf16[64,8,256]{2,0,1:T(8,128)(2,1)S(1)} %bitcast.151), channel_id=1, replica_groups=mesh['uly'=8,'blk'=32] {'uly'}, dimensions={1} | all-to-all | bytes 524288 | tf_op jit(solution)/shard_map/all_to_all | solution.py:41
  32.1 4.5 %all-to-all-done = bf16[64,8,256]{2,0,1:T(8,128)(2,1)S(1)} async-done(((bf16[64,8,256]{2,0,1:T(8,128)(2,1)}), bf16[64,8,256]{2,0,1:T(8,128)(2,1)S(1)}, u32[]{:S(2)}, u32[]{:S(2)}) %all-to-all-start) | async-done | bytes 262176 | tf_op jit(solution)/shard_map/all_to_all | solution.py:40
  41.1 9.5 %all-to-all-done.2 = bf16[64,8,256]{2,0,1:T(8,128)(2,1)S(1)} async-done(((bf16[64,8,256]{2,0,1:T(8,128)(2,1)}), bf16[64,8,256]{2,0,1:T(8,128)(2,1)S(1)}, u32[]{:S(2)}, u32[]{:S(2)}) %all-to-all-start.2) | async-done | bytes 262176 | tf_op jit(solution)/shard_map/all_to_all | solution.py:42
  50.7 42.7 %all-gather.2.cloned.1.call-done = bf16[16384,256]{1,0:T(8,128)(2,1)} async-done(((bf16[512,256]{1,0:T(8,128)(2,1)}), bf16[16384,256]{1,0:T(8,128)(2,1)}) %all-gather.2.cloned.1.call-update) | async-done | bytes 8388624 | tf_op jit(solution)/shard_map/all_gather | solution.py:44
  93.3 13.5 %reshape.301 = bf16[256,16384]{1,0:T(8,128)(2,1)} reshape(bf16[16384,256]{1,0:T(8,128)(2,1)} %all-gather.2.cloned.1.call-done) | data formatting | bytes 16777216 | tf_op jit(solution)/shard_map/reshape | solution.py:82
  106.8 124.2 %while.16 = (s32[]{:T(128)}, f32[256,16384]{1,0:T(8,128)}, bf16[2,8,64,128]{3,2,1,0:T(8,128)(2,1)S(1)}, bf16[2,8,64,128]{3,2,1,0:T(8,128)(2,1)S(1)}, s32[2,8,16]...) while((s32[]{:T(128)}, f32[256,16384]{1,0:T(8,128)}, ...), condition=%wide.region_5.6_spmd.clone, body=%wide.region_1.5_spmd.clone.sunk | while | flops 8343976960 | bytes 164273328 | solution.py:149
  106.9 6.7 %convolution_convert_fusion.2 = bf16[128,16384]{1,0:T(8,128)(2,1)} fusion(bf16[256,16384]{1,0:T(8,128)(2,1)} %get-tuple-element.291, s32[128]{0:T(128)S(1)} %eq.82), kind=kOutput, calls=%fused_computation.3.clone.1 | convolution fusion | flops 1075871744 | bytes 12583424 | tf_op jit(solution)/shard_map/while/body/eval_jaxpr/dot_general | solution.py:92
  113.5 7.4 %reshape.329 = bf16[8,1024,256]{2,1,0:T(8,128)(2,1)} reshape(bf16[128,16384]{1,0:T(8,128)(2,1)} %convolution_convert_fusion.2) | data formatting | bytes 8388608 | tf_op jit(solution)/shard_map/while/body/eval_jaxpr/reshape | solution.py:94
  128.1 4.1 pad_maximum_fusion.3
  132.2 9.1 %copy.125 = f32[8,1024,256]{2,1,0:T(8,128)} copy(f32[8,1024,256]{1,2,0:T(8,128)} %pad_maximum_fusion.3) | data formatting | bytes 16777216 | tf_op jit(solution)/shard_map/while/body/eval_jaxpr/concatenate | solution.py:129
  141.3 9.4 %reshape.330 = f32[128,16384]{1,0:T(8,128)} reshape(f32[8,1024,256]{2,1,0:T(8,128)} %copy.125) | data formatting | bytes 16777216 | tf_op jit(solution)/shard_map/while/body/eval_jaxpr/reshape | solution.py:129
  150.7 17.0 %convolution_add_fusion.2 = f32[256,16384]{1,0:T(8,128)} fusion(f32[128,16384]{1,0:T(8,128)} %reshape.330, f32[256,16384]{1,0:T(8,128)} %get-tuple-element.274, pred[]{:T(512)S(6)} %compare.31, s32[128]{0:T(128)S(1)} %eq.82), kind=kOutput, calls=%fused_computation.2.clone.1 | convolution fusion | flops 6450872320 | bytes 41943552 | tf_op jit(solution)/shard_map/while/body/eval_jaxpr/dot_general | solution.py:133
  167.8 6.7 %convolution_convert_fusion.2 = bf16[128,16384]{1,0:T(8,128)(2,1)} fusion(bf16[256,16384]{1,0:T(8,128)(2,1)} %get-tuple-element.291, s32[128]{0:T(128)S(1)} %eq.82), kind=kOutput, calls=%fused_computation.3.clone.1 | convolution fusion | flops 1075871744 | bytes 12583424 | tf_op jit(solution)/shard_map/while/body/eval_jaxpr/dot_general | solution.py:92
  174.4 7.4 %reshape.329 = bf16[8,1024,256]{2,1,0:T(8,128)(2,1)} reshape(bf16[128,16384]{1,0:T(8,128)(2,1)} %convolution_convert_fusion.2) | data formatting | bytes 8388608 | tf_op jit(solution)/shard_map/while/body/eval_jaxpr/reshape | solution.py:94
  189.0 4.1 pad_maximum_fusion.3
  193.1 9.1 %copy.125 = f32[8,1024,256]{2,1,0:T(8,128)} copy(f32[8,1024,256]{1,2,0:T(8,128)} %pad_maximum_fusion.3) | data formatting | bytes 16777216 | tf_op jit(solution)/shard_map/while/body/eval_jaxpr/concatenate | solution.py:129
  202.2 9.4 %reshape.330 = f32[128,16384]{1,0:T(8,128)} reshape(f32[8,1024,256]{2,1,0:T(8,128)} %copy.125) | data formatting | bytes 16777216 | tf_op jit(solution)/shard_map/while/body/eval_jaxpr/reshape | solution.py:129
  211.6 19.4 %convolution_add_fusion.2 = f32[256,16384]{1,0:T(8,128)} fusion(f32[128,16384]{1,0:T(8,128)} %reshape.330, f32[256,16384]{1,0:T(8,128)} %get-tuple-element.274, pred[]{:T(512)S(6)} %compare.31, s32[128]{0:T(128)S(1)} %eq.82), kind=kOutput, calls=%fused_computation.2.clone.1 | convolution fusion | flops 6450872320 | bytes 41943552 | tf_op jit(solution)/shard_map/while/body/eval_jaxpr/dot_general | solution.py:133
  231.0 18.0 %reshape.310 = f32[16384,256]{1,0:T(8,128)} reshape(f32[256,16384]{1,0:T(8,128)} %get-tuple-element.86) | data formatting | bytes 33554432 | tf_op jit(solution)/shard_map/reshape | solution.py:150
  252.9 6.9 %all-to-all-start.4 = ((bf16[8,2,8192]{2,1,0:T(2,128)(2,1)}), bf16[8,2,8192]{2,1,0:T(2,128)(2,1)S(1)}, u32[]{:S(2)}, u32[]{:S(2)}) async-start(bf16[8,2,8192]{2,1,0:T(2,128)(2,1)} %reshape.325), calls=%async_computation.4 | async-start | bytes 524288 | tf_op jit(solution)/shard_map/all_to_all | solution.py:165
  263.2 11.2 %all-to-all-done.4 = bf16[8,2,8192]{2,1,0:T(2,128)(2,1)S(1)} async-done(((bf16[8,2,8192]{2,1,0:T(2,128)(2,1)}), bf16[8,2,8192]{2,1,0:T(2,128)(2,1)S(1)}, u32[]{:S(2)}, u32[]{:S(2)}) %all-to-all-start.4) | async-done | bytes 262176 | tf_op jit(solution)/shard_map/all_to_all | solution.py:165
  277.8 115.9 %reduce-scatter.2.cloned.1.call-done = f32[512,256]{1,0:T(8,128)} async-done(((f32[16384,256]{1,0:T(8,128)}), f32[512,256]{1,0:T(8,128)}) %reduce-scatter.2.cloned.1.call-update) | async-done | bytes 524304 | tf_op jit(solution)/shard_map/reduce_scatter | solution.py:169
  396.0 6.3 %all-to-all-start.5 = ((f32[512,1,256]{2,1,0:T(1,128)}), f32[512,1,256]{2,1,0:T(1,128)S(1)}, u32[]{:S(2)}, u32[]{:S(2)}) async-start(f32[512,1,256]{2,1,0:T(1,128)} %reshape.311), calls=%async_computation.6 | async-start | bytes 1048576 | tf_op jit(solution)/shard_map/all_to_all | solution.py:170
  404.3 7.7 %all-to-all-done.5 = f32[512,1,256]{2,1,0:T(1,128)S(1)} async-done(((f32[512,1,256]{2,1,0:T(1,128)}), f32[512,1,256]{2,1,0:T(1,128)S(1)}, u32[]{:S(2)}, u32[]{:S(2)}) %all-to-all-start.5) | async-done | bytes 524320 | tf_op jit(solution)/shard_map/all_to_all | solution.py:170
  (93 shorter events, 45.7 us)
Async XLA Ops:
  7.2 86.2 %all-gather.2.cloned.1.call-start = ((), (), s32[]{:S(2)}) async-start(), calls=%async_computation.7 | async-start | bytes 8650752 | tf_op jit(solution)/shard_map/all_gather | solution.py:44
  24.4 12.1 %all-to-all-start = ((bf16[64,8,256]{2,0,1:T(8,128)(2,1)}), bf16[64,8,256]{2,0,1:T(8,128)(2,1)S(1)}, u32[]{:S(2)}, u32[]{:S(2)}) async-start(bf16[64,8,256]{2,0,1:T(8,128)(2,1)} %bitcast.115), calls=%async_computation | async-start | bytes 524288 | tf_op jit(solution)/shard_map/all_to_all | solution.py:40
  36.5 14.0 %all-to-all-start.2 = ((bf16[64,8,256]{2,0,1:T(8,128)(2,1)}), bf16[64,8,256]{2,0,1:T(8,128)(2,1)S(1)}, u32[]{:S(2)}, u32[]{:S(2)}) async-start(bf16[64,8,256]{2,0,1:T(8,128)(2,1)} %bitcast.114), calls=%async_computation.2 | async-start | bytes 524288 | tf_op jit(solution)/shard_map/all_to_all | solution.py:42
  39.9 353.8 %reduce-scatter.2.cloned.1.call-start = ((), (), s32[]{:S(2)}) async-start(), calls=%async_computation.8 | async-start | bytes 17301504 | tf_op jit(solution)/shard_map/reduce_scatter | solution.py:169
  120.9 3.3 copy-start
  181.8 3.3 copy-start
  252.9 21.5 %all-to-all-start.4 = ((bf16[8,2,8192]{2,1,0:T(2,128)(2,1)}), bf16[8,2,8192]{2,1,0:T(2,128)(2,1)S(1)}, u32[]{:S(2)}, u32[]{:S(2)}) async-start(bf16[8,2,8192]{2,1,0:T(2,128)(2,1)} %reshape.325), calls=%async_computation.4 | async-start | bytes 524288 | tf_op jit(solution)/shard_map/all_to_all | solution.py:165
  274.4 121.5 %all-to-all-start.3 = ((bf16[8,2,8192]{2,1,0:T(2,128)(2,1)}), bf16[8,2,8192]{2,1,0:T(2,128)(2,1)S(1)}, u32[]{:S(2)}, u32[]{:S(2)}) async-start(bf16[8,2,8192]{2,1,0:T(2,128)(2,1)} %reshape.323), calls=%async_computation.3 | async-start | bytes 524288 | tf_op jit(solution)/shard_map/all_to_all | solution.py:164
  396.0 16.0 %all-to-all-start.5 = ((f32[512,1,256]{2,1,0:T(1,128)}), f32[512,1,256]{2,1,0:T(1,128)S(1)}, u32[]{:S(2)}, u32[]{:S(2)}) async-start(f32[512,1,256]{2,1,0:T(1,128)} %reshape.311), calls=%async_computation.6 | async-start | bytes 1048576 | tf_op jit(solution)/shard_map/all_to_all | solution.py:170
Sparse Core Ops, SparseCore 0:
  22.9 70.4 all-gather.1
  249.1 144.5 reduce-scatter.1
where the time goes:
time: 422 us; the launch traced here: 420 us
  waiting for transfers between devices  191 us (45%)
  local copies, waits for them, and re-layouts  98.5 us (23%)
  matrix products  62.6 us (15%)
  starting transfers between devices  23.5 us (6%)
  other arithmetic  15.2 us (4%)
  between operations  14.3 us (3%)
  blocking collectives  13.9 us (3%)
    reduce_scatter x1, waiting for transfers between devices, body(): lax.psum_scatter(kv_grad_all, 'blk', scatter_dimension=0, tiled=True)  116 us
    all_gather x1, waiting for transfers between devices, body(): keys_all = lax.all_gather(kv_mine[:, 0, :], 'blk', axis=0, tiled=True)  42.7 us
    dot_general x2, matrix products, group_step(): jnp.dot(place_table.T, both_parts, preferred_element_type=jnp.float32, pr...  36.4 us
    reshape x2, local copies, waits for them, and re-layouts, group_step(): jnp.concatenate([key_portion, value_portion], axis=2)  18.8 us
    concatenate x2, local copies, waits for them, and re-layouts, group_step(): jnp.concatenate([key_portion, value_portion], axis=2)  18.2 us
    reshape x1, local copies, waits for them, and re-layouts, body(): kv_grad_all = unit_grads.reshape(total_tokens, 2 * HEAD_SIZE)  18 us
    reshape x2, local copies, waits for them, and re-layouts, group_step(): gathered = jnp.dot(fetch_table, keys_units, preferred_element_type=jnp.fl...  14.8 us
    all_to_all x1, blocking collectives, body(): lax.all_to_all(kv_slots, 'uly', split_axis=1, concat_axis=0, tiled=True)  13.9 us
  transfers between devices with their start and end apart: 7, of which 6 were waited for; matrix products, arithmetic and copies ran while one was open for 4% of the time, Pallas kernels for 0%

commit v1 on v0

--- a/solution.py
+++ b/solution.py
@@ -41,7 +41,16 @@
         lax.all_to_all(kv_slots, "uly", split_axis=1, concat_axis=0, tiled=True),
         lax.all_to_all(grad_slots, "uly", split_axis=1, concat_axis=0, tiled=True),
     )
-    keys_all = lax.all_gather(kv_mine[:, 0, :], "blk", axis=0, tiled=True)
+    vec = kv_mine[:, 0, :]
+    keys_all = jnp.concatenate(
+        lax.all_to_all(
+            jnp.stack([vec for _ in range(lax.axis_size("blk"))]),
+            axis_name="blk",
+            split_axis=0,
+            concat_axis=0,
+        ),
+        0,
+    )
     item_count = heads_dev * ulysses_width * sub_count
     query_items = (
         query_all.reshape(ulysses_width, sub_count, sub_length, heads_dev, HEAD_SIZE)

time: 422 us -> 574 us (1.36)
  waiting for transfers between devices: 191 us -> 334 us
  starting transfers between devices: 23.5 us -> 30.6 us
    all_to_all x1 -> x2, waiting for transfers between devices: 9.48 us -> 190 us  [the longest x1 183 us: body(): lax.all_to_all(jnp.stack([vec for _ in range(lax.axis_size('blk'))]), axi...]
    all_gather x1 -> x0, waiting for transfers between devices: 42.7 us -> none  [body(): keys_all = lax.all_gather(kv_mine[:, 0, :], 'blk', axis=0, tiled=True)]
    another operation x0 -> x2, local copies, waits for them, and re-layouts: none -> 17.6 us  [the longest x1 13.5 us: body(): keys_units = keys_all.reshape(units_total, unit_len * 2 * HEAD_SIZE)]
    reshape x1 -> x0, local copies, waits for them, and re-layouts: 13.5 us -> none  [body(): keys_units = keys_all.reshape(units_total, unit_len * 2 * HEAD_SIZE)]
    all_to_all x1 -> x2, starting transfers between devices: 3.41 us -> 14.4 us  [the longest x1 9.15 us: body(): lax.all_to_all(jnp.stack([vec for _ in range(lax.axis_size('blk'))]), axi...]
    reduce_scatter x1, waiting for transfers between devices: 116 us -> 124 us  [body(): lax.psum_scatter(kv_grad_all, 'blk', scatter_dimension=0, tiled=True)]
    all_to_all x1, waiting for transfers between devices: 11.2 us -> 5.29 us  [body(): lax.all_to_all(qgrad_items, 'uly', split_axis=0, concat_axis=1, tiled=True)]
  transfers between devices with their start and end apart: 7 -> 7, of which waited for: 6 -> 6; matrix products, arithmetic and copies ran while one was open for 4% -> 3% of each run, Pallas kernels for 0% -> 0%
where the time goes in v1:
time: 574 us; the launch traced here: 570 us
  waiting for transfers between devices  334 us (58%)
  local copies, waits for them, and re-layouts  102 us (18%)
  matrix products  62.6 us (11%)
  starting transfers between devices  30.6 us (5%)
  other arithmetic  15.3 us (3%)
  between operations  14.3 us (2%)
  blocking collectives  11.3 us (2%)
    all_to_all x1, waiting for transfers between devices, body(): lax.all_to_all(jnp.stack([vec for _ in range(lax.axis_size('blk'))]), axi...  183 us
    reduce_scatter x1, waiting for transfers between devices, body(): lax.psum_scatter(kv_grad_all, 'blk', scatter_dimension=0, tiled=True)  124 us
    dot_general x2, matrix products, group_step(): jnp.dot(place_table.T, both_parts, preferred_element_type=jnp.float32, pr...  36.4 us
    reshape x2, local copies, waits for them, and re-layouts, group_step(): jnp.concatenate([key_portion, value_portion], axis=2)  18.8 us
    concatenate x2, local copies, waits for them, and re-layouts, group_step(): jnp.concatenate([key_portion, value_portion], axis=2)  18.2 us
    reshape x1, local copies, waits for them, and re-layouts, body(): kv_grad_all = unit_grads.reshape(total_tokens, 2 * HEAD_SIZE)  18 us
    reshape x2, local copies, waits for them, and re-layouts, group_step(): gathered = jnp.dot(fetch_table, keys_units, preferred_element_type=jnp.fl...  14.8 us
    another operation x1, local copies, waits for them, and re-layouts, body(): keys_units = keys_all.reshape(units_total, unit_len * 2 * HEAD_SIZE)  13.5 us
  transfers between devices with their start and end apart: 7, of which 6 were waited for; matrix products, arithmetic and copies ran while one was open for 3% of the time, Pallas kernels for 0%

profile of v1, /device:TPU:0, one launch (start us, length us, event | category | flops | bytes accessed | tf_op | source)
XLA Modules:
  0.0 570.4 jit_solution(607451402119821147)
XLA Ops:
  9.5 5.2 all-to-all-start.1
  16.4 7.1 %all-to-all-done.1 = bf16[64,8,256]{2,0,1:T(8,128)(2,1)S(1)} async-done(((bf16[64,8,256]{2,0,1:T(8,128)(2,1)}), bf16[64,8,256]{2,0,1:T(8,128)(2,1)S(1)}, u32[]{:S(2)}, u32[]{:S(2)}) %all-to-all-start.1) | async-done | bytes 262176 | tf_op jit(solution)/shard_map/all_to_all | solution.py:41
  27.9 7.7 %all-to-all-done = bf16[64,8,256]{2,0,1:T(8,128)(2,1)S(1)} async-done(((bf16[64,8,256]{2,0,1:T(8,128)(2,1)}), bf16[64,8,256]{2,0,1:T(8,128)(2,1)S(1)}, u32[]{:S(2)}, u32[]{:S(2)}) %all-to-all-start) | async-done | bytes 262176 | tf_op jit(solution)/shard_map/all_to_all | solution.py:40
  35.6 11.3 %all_to_all.95 = bf16[64,8,256]{2,0,1:T(8,128)(2,1)S(1)} all-to-all(bf16[64,8,256]{2,0,1:T(8,128)(2,1)S(1)} %bitcast.154), channel_id=1, replica_groups=mesh['uly'=8,'blk'=32] {'uly'}, dimensions={1} | all-to-all | bytes 524288 | tf_op jit(solution)/shard_map/all_to_all | solution.py:42
  46.8 4.2 stack.3
  51.0 9.1 %all-to-all-start.2 = ((bf16[32,512,256]{2,1,0:T(8,128)(2,1)}), bf16[32,512,256]{2,1,0:T(8,128)(2,1)}, u32[]{:S(2)}, u32[]{:S(2)}) async-start(bf16[32,512,256]{2,1,0:T(8,128)(2,1)} %stack.3), calls=%async_computation.2 | async-start | bytes 16777216 | tf_op jit(solution)/shard_map/all_to_all | solution.py:46
  63.3 183.0 %all-to-all-done.2 = bf16[32,512,256]{2,1,0:T(8,128)(2,1)} async-done(((bf16[32,512,256]{2,1,0:T(8,128)(2,1)}), bf16[32,512,256]{2,1,0:T(8,128)(2,1)}, u32[]{:S(2)}, u32[]{:S(2)}) %all-to-all-start.2) | async-done | bytes 8388640 | tf_op jit(solution)/shard_map/all_to_all | solution.py:46
  246.3 13.5 %reshape_reshape.10 = bf16[256,16384]{1,0:T(8,128)(2,1)} reshape(bf16[32,512,256]{2,1,0:T(8,128)(2,1)} %all-to-all-done.2) | data formatting | bytes 16777216 | tf_op jit(solution)/shard_map/reshape;reshape | solution.py:91
  259.8 124.2 %while.16 = (s32[]{:T(128)}, f32[256,16384]{1,0:T(8,128)}, bf16[2,8,64,128]{3,2,1,0:T(8,128)(2,1)S(1)}, bf16[2,8,64,128]{3,2,1,0:T(8,128)(2,1)S(1)}, s32[2,8,16]...) while((s32[]{:T(128)}, f32[256,16384]{1,0:T(8,128)}, ...), condition=%wide.region_5.6_spmd.clone, body=%wide.region_1.5_spmd.clone.sunk | while | flops 8343976960 | bytes 164273328 | solution.py:158
  259.8 6.7 %convolution_convert_fusion.2 = bf16[128,16384]{1,0:T(8,128)(2,1)} fusion(bf16[256,16384]{1,0:T(8,128)(2,1)} %get-tuple-element.291, s32[128]{0:T(128)S(1)} %eq.82), kind=kOutput, calls=%fused_computation.3.clone.1 | convolution fusion | flops 1075871744 | bytes 12583424 | tf_op jit(solution)/shard_map/while/body/eval_jaxpr/dot_general | solution.py:101
  266.5 7.4 %reshape.327 = bf16[8,1024,256]{2,1,0:T(8,128)(2,1)} reshape(bf16[128,16384]{1,0:T(8,128)(2,1)} %convolution_convert_fusion.2) | data formatting | bytes 8388608 | tf_op jit(solution)/shard_map/while/body/eval_jaxpr/reshape | solution.py:103
  285.1 9.1 %copy.125 = f32[8,1024,256]{2,1,0:T(8,128)} copy(f32[8,1024,256]{1,2,0:T(8,128)} %pad_maximum_fusion.3) | data formatting | bytes 16777216 | tf_op jit(solution)/shard_map/while/body/eval_jaxpr/concatenate | solution.py:138
  294.3 9.4 %reshape.328 = f32[128,16384]{1,0:T(8,128)} reshape(f32[8,1024,256]{2,1,0:T(8,128)} %copy.125) | data formatting | bytes 16777216 | tf_op jit(solution)/shard_map/while/body/eval_jaxpr/reshape | solution.py:138
  303.6 17.0 %convolution_add_fusion.2 = f32[256,16384]{1,0:T(8,128)} fusion(f32[128,16384]{1,0:T(8,128)} %reshape.328, f32[256,16384]{1,0:T(8,128)} %get-tuple-element.274, pred[]{:T(512)S(6)} %compare.31, s32[128]{0:T(128)S(1)} %eq.82), kind=kOutput, calls=%fused_computation.2.clone.1 | convolution fusion | flops 6450872320 | bytes 41943552 | tf_op jit(solution)/shard_map/while/body/eval_jaxpr/dot_general | solution.py:142
  320.7 6.7 %convolution_convert_fusion.2 = bf16[128,16384]{1,0:T(8,128)(2,1)} fusion(bf16[256,16384]{1,0:T(8,128)(2,1)} %get-tuple-element.291, s32[128]{0:T(128)S(1)} %eq.82), kind=kOutput, calls=%fused_computation.3.clone.1 | convolution fusion | flops 1075871744 | bytes 12583424 | tf_op jit(solution)/shard_map/while/body/eval_jaxpr/dot_general | solution.py:101
  327.4 7.4 %reshape.327 = bf16[8,1024,256]{2,1,0:T(8,128)(2,1)} reshape(bf16[128,16384]{1,0:T(8,128)(2,1)} %convolution_convert_fusion.2) | data formatting | bytes 8388608 | tf_op jit(solution)/shard_map/while/body/eval_jaxpr/reshape | solution.py:103
  346.0 9.1 %copy.125 = f32[8,1024,256]{2,1,0:T(8,128)} copy(f32[8,1024,256]{1,2,0:T(8,128)} %pad_maximum_fusion.3) | data formatting | bytes 16777216 | tf_op jit(solution)/shard_map/while/body/eval_jaxpr/concatenate | solution.py:138
  355.1 9.4 %reshape.328 = f32[128,16384]{1,0:T(8,128)} reshape(f32[8,1024,256]{2,1,0:T(8,128)} %copy.125) | data formatting | bytes 16777216 | tf_op jit(solution)/shard_map/while/body/eval_jaxpr/reshape | solution.py:138
  364.5 19.4 %convolution_add_fusion.2 = f32[256,16384]{1,0:T(8,128)} fusion(f32[128,16384]{1,0:T(8,128)} %reshape.328, f32[256,16384]{1,0:T(8,128)} %get-tuple-element.274, pred[]{:T(512)S(6)} %compare.31, s32[128]{0:T(128)S(1)} %eq.82), kind=kOutput, calls=%fused_computation.2.clone.1 | convolution fusion | flops 6450872320 | bytes 41943552 | tf_op jit(solution)/shard_map/while/body/eval_jaxpr/dot_general | solution.py:142
  383.9 18.0 %reshape.308 = f32[16384,256]{1,0:T(8,128)} reshape(f32[256,16384]{1,0:T(8,128)} %get-tuple-element.86) | data formatting | bytes 33554432 | tf_op jit(solution)/shard_map/reshape | solution.py:159
  412.7 5.3 all-to-all-done.5
  421.4 123.5 %reduce-scatter.2.cloned.1.call-done = f32[512,256]{1,0:T(8,128)} async-done(((f32[16384,256]{1,0:T(8,128)}), f32[512,256]{1,0:T(8,128)}) %reduce-scatter.2.cloned.1.call-update) | async-done | bytes 524304 | tf_op jit(solution)/shard_map/reduce_scatter | solution.py:178
  547.1 5.9 %all-to-all-start.6 = ((f32[512,1,256]{2,1,0:T(1,128)}), f32[512,1,256]{2,1,0:T(1,128)S(1)}, u32[]{:S(2)}, u32[]{:S(2)}) async-start(f32[512,1,256]{2,1,0:T(1,128)} %reshape.309), calls=%async_computation.7 | async-start | bytes 1048576 | tf_op jit(solution)/shard_map/all_to_all | solution.py:179
  555.2 7.7 %all-to-all-done.6 = f32[512,1,256]{2,1,0:T(1,128)S(1)} async-done(((f32[512,1,256]{2,1,0:T(1,128)}), f32[512,1,256]{2,1,0:T(1,128)S(1)}, u32[]{:S(2)}, u32[]{:S(2)}) %all-to-all-start.6) | async-done | bytes 524320 | tf_op jit(solution)/shard_map/all_to_all | solution.py:179
  (95 shorter events, 53.1 us)
Async XLA Ops:
  9.5 14.0 %all-to-all-start.1 = ((bf16[64,8,256]{2,0,1:T(8,128)(2,1)}), bf16[64,8,256]{2,0,1:T(8,128)(2,1)S(1)}, u32[]{:S(2)}, u32[]{:S(2)}) async-start(bf16[64,8,256]{2,0,1:T(8,128)(2,1)} %bitcast.6), calls=%async_computation.1 | async-start | bytes 524288 | tf_op jit(solution)/shard_map/all_to_all | solution.py:41
  23.5 12.1 %all-to-all-start = ((bf16[64,8,256]{2,0,1:T(8,128)(2,1)}), bf16[64,8,256]{2,0,1:T(8,128)(2,1)S(1)}, u32[]{:S(2)}, u32[]{:S(2)}) async-start(bf16[64,8,256]{2,0,1:T(8,128)(2,1)} %bitcast.115), calls=%async_computation | async-start | bytes 524288 | tf_op jit(solution)/shard_map/all_to_all | solution.py:40
  51.0 9.3 %copy-start.1 = (s32[2,128,8]{1,2,0:T(8,128)S(1)}, s32[2,128,8]{1,2,0:T(8,128)}, u32[]{:S(2)}) copy-start(s32[2,128,8]{1,2,0:T(8,128)} %param.11) | copy-start | bytes 24580
  51.0 195.3 %all-to-all-start.2 = ((bf16[32,512,256]{2,1,0:T(8,128)(2,1)}), bf16[32,512,256]{2,1,0:T(8,128)(2,1)}, u32[]{:S(2)}, u32[]{:S(2)}) async-start(bf16[32,512,256]{2,1,0:T(8,128)(2,1)} %stack.3), calls=%async_computation.2 | async-start | bytes 16777216 | tf_op jit(solution)/shard_map/all_to_all | solution.py:46
  60.2 484.8 %reduce-scatter.2.cloned.1.call-start = ((), (), s32[]{:S(2)}) async-start(), calls=%async_computation.8 | async-start | bytes 17301504 | tf_op jit(solution)/shard_map/reduce_scatter | solution.py:178
  273.9 3.3 copy-start
  334.8 3.3 copy-start
  405.9 12.1 %all-to-all-start.5 = ((bf16[8,2,8192]{2,1,0:T(2,128)(2,1)}), bf16[8,2,8192]{2,1,0:T(2,128)(2,1)S(1)}, u32[]{:S(2)}, u32[]{:S(2)}) async-start(bf16[8,2,8192]{2,1,0:T(2,128)(2,1)} %reshape.323), calls=%async_computation.5 | async-start | bytes 524288 | tf_op jit(solution)/shard_map/all_to_all | solution.py:174
  418.0 129.1 %all-to-all-start.4 = ((bf16[8,2,8192]{2,1,0:T(2,128)(2,1)}), bf16[8,2,8192]{2,1,0:T(2,128)(2,1)S(1)}, u32[]{:S(2)}, u32[]{:S(2)}) async-start(bf16[8,2,8192]{2,1,0:T(2,128)(2,1)} %reshape.321), calls=%async_computation.4 | async-start | bytes 524288 | tf_op jit(solution)/shard_map/all_to_all | solution.py:173
  547.1 15.7 %all-to-all-start.6 = ((f32[512,1,256]{2,1,0:T(1,128)}), f32[512,1,256]{2,1,0:T(1,128)S(1)}, u32[]{:S(2)}, u32[]{:S(2)}) async-start(f32[512,1,256]{2,1,0:T(1,128)} %reshape.309), calls=%async_computation.7 | async-start | bytes 1048576 | tf_op jit(solution)/shard_map/all_to_all | solution.py:179
Sparse Core Ops, SparseCore 0:
  402.1 142.8 reduce-scatter.1
